TPU v7x, 32 devices: a whole 2x2x4 slice. The times are simulated.
32 devices in a mesh: scene: 2 (over x), view: 16 (over z, y, core).
Axes of the slice: x: 2, y: 2, z: 4, core: 2. Of those that a mesh axis runs over, the one named last changes fastest.
Arguments:
- src_feat: bfloat16 [32, 32, 8192], P(('scene', 'view')), parts along dimension 0, may hold values from -6 to 6
- ref_feat: bfloat16 [32, 32, 512], P(('scene', 'view')), parts along dimension 0, may hold values from -6 to 6
- weight_table: bfloat16 [4, 128, 512], replicated, may hold values from -0.5 to 0.5
- src_block: int32 [32, 64, 4], P(('scene', 'view')), parts along dimension 0, may hold values from 0 to 63
- table_index: int32 [32, 64, 4], P(('scene', 'view')), parts along dimension 0, may hold values from 0 to 3, each once within a row
- block_count: int32 [32, 64], P(('scene', 'view')), parts along dimension 0, may hold values from 0 to 4, as said below
- depth_plane: int32 [32, 64], P(('scene', 'view')), parts along dimension 0, may hold values from 0 to 63
- kern_one: bfloat16 [3, 3, 3, 8, 8], replicated, may hold values from -0.4375 to 0.4375
- kern_two: bfloat16 [3, 3, 3, 8], replicated, may hold values from -0.4375 to 0.4375
Outputs:
- depth_score: float32 [128, 64, 128], P(('scene', 'view')), parts along dimension 0
There are 2 independent parts, one for each index of `scene`. A program takes and returns all parts, laid end to end along the dimension named above; an argument that names none is the same for every part. Nothing has to cross between parts.
Inputs may be any that keep to these rules, and one draw needn't show every extreme that they name: `block_count`: each entry is the number of live block slots of a unit, 0 for an empty unit; the share of live units differs between source views. `table_index`: the 4 table indices of a unit are distinct.
All inputs are finite; a program needn't handle non-finite values.
Results may differ from a plain program's by a relative error of at most 0.019.
Values may be sent and summed in bfloat16 or wider, within the bound.
No kernel may reach another device: no remote copies, remote signals or barrier semaphores. Data moves between devices by JAX's collectives and lax.ppermute only.
A program may use at most 128 MiB of HBM per device.

v0:
```python
import jax
import jax.numpy as jnp
from jax import lax
from jax.sharding import PartitionSpec as P

GROUPS = 8
DEPTH = 64
TROWS = 4


def with_halo(block, sides, width):
    for axis, dim in sides:
        count = lax.axis_size(axis)
        forward = [(i, i + 1) for i in range(count - 1)]
        backward = [(target, source) for source, target in forward]
        low = lax.ppermute(
            lax.slice_in_dim(block, block.shape[dim] - width, None, axis=dim), axis, forward
        )
        high = lax.ppermute(lax.slice_in_dim(block, 0, width, axis=dim), axis, backward)
        block = jnp.concatenate([low, block, high], axis=dim)
    return block


def convolve_full(padded, kernel):
    rows_out = padded.shape[0] - 2
    depth_len = padded.shape[2]
    columns = padded.shape[3]
    framed = jnp.pad(padded, ((0, 0), (0, 0), (1, 1), (1, 1)))
    carried = jnp.zeros((rows_out, kernel.shape[-1], depth_len, columns), jnp.float32)
    for depth_off in range(3):
        for row_off in range(3):
            for col_off in range(3):
                window = framed[
                    row_off : row_off + rows_out,
                    :,
                    depth_off : depth_off + depth_len,
                    col_off : col_off + columns,
                ]
                carried = carried + jnp.einsum(
                    "rcdw,ce->redw",
                    window,
                    kernel[depth_off, row_off, col_off],
                    preferred_element_type=jnp.float32,
                )
    return carried


def convolve_final(padded, kernel):
    rows_out = padded.shape[0] - 2
    depth_len = padded.shape[2]
    columns = padded.shape[3]
    framed = jnp.pad(padded, ((0, 0), (0, 0), (1, 1), (1, 1)))
    carried = jnp.zeros((rows_out, depth_len, columns), jnp.float32)
    for depth_off in range(3):
        for row_off in range(3):
            for col_off in range(3):
                window = framed[
                    row_off : row_off + rows_out,
                    :,
                    depth_off : depth_off + depth_len,
                    col_off : col_off + columns,
                ]
                carried = carried + jnp.einsum(
                    "rcdw,c->rdw",
                    window,
                    kernel[depth_off, row_off, col_off],
                    preferred_element_type=jnp.float32,
                )
    return carried


def pad_rows(volume):
    return with_halo(volume, (("view", 0),), 1)


def body(
    src_feat,
    ref_feat,
    weight_table,
    src_block,
    table_index,
    block_count,
    depth_plane,
    kern_one,
    kern_two,
):
    owners = lax.axis_size("view")
    features = src_feat[0]
    channels, spix = features.shape
    slots, block_width, tpix = weight_table.shape
    blocks = features.reshape(channels, spix // block_width, block_width).transpose(1, 0, 2)
    units = src_block.shape[1]
    cap = units // owners
    counts = block_count[0]
    live_slot = jnp.arange(slots)[None, :] < counts[:, None]
    chosen = (
        (table_index[0][:, :, None] == jnp.arange(slots)[None, None, :]) & live_slot[:, :, None]
    ).astype(jnp.bfloat16)
    depth_code = jnp.where(counts > 0, depth_plane[0], -1).astype(jnp.bfloat16)
    unit_rounds = 8
    per_round = units // unit_rounds
    index_groups = src_block[0].reshape(unit_rounds, per_round, slots)
    chosen_groups = chosen.reshape(unit_rounds, per_round, slots, slots)
    group_size = channels // GROUPS
    ref_all = lax.all_to_all(
        jnp.broadcast_to(ref_feat, (owners,) + ref_feat.shape[1:]),
        "view",
        split_axis=0,
        concat_axis=0,
        tiled=True,
    )

    def resample(index_rows, chosen_rows):
        gathered = blocks[index_rows]
        arranged = jnp.einsum(
            "ujw,ujck->uwck", chosen_rows, gathered, preferred_element_type=jnp.float32
        ).astype(jnp.bfloat16)
        return jnp.einsum(
            "uwck,wkp->ucp", arranged, weight_table, preferred_element_type=jnp.float32
        ).astype(jnp.bfloat16)

    warped_all = lax.map(
        lambda packed: resample(packed[0], packed[1]), (index_groups, chosen_groups)
    ).reshape(owners, cap, channels, tpix)
    products = ref_all.astype(jnp.float32)[:, None] * warped_all.astype(jnp.float32)
    corr_all = (
        (products.reshape(units, GROUPS, group_size, tpix).sum(axis=2) * (GROUPS / channels))
        .astype(jnp.bfloat16)
        .reshape(units, GROUPS * tpix)
    )
    tag_lanes = jnp.broadcast_to(depth_code[:, None], (units, 128))
    payload = jnp.concatenate([corr_all, tag_lanes], axis=1)
    arriving = lax.all_to_all(
        payload.reshape(owners, cap, GROUPS * tpix + 128),
        "view",
        split_axis=0,
        concat_axis=0,
        tiled=True,
    ).reshape(owners * cap, GROUPS * tpix + 128)
    received = arriving[:, : GROUPS * tpix]
    depth_tags = arriving[:, GROUPS * tpix]
    onehot = (depth_tags[None, :] == jnp.arange(DEPTH).astype(jnp.bfloat16)[:, None]).astype(
        jnp.bfloat16
    )
    summed = jnp.dot(onehot, received, preferred_element_type=jnp.float32)
    tallies = jnp.sum(onehot.astype(jnp.float32), axis=1)
    cost_volume = (summed / jnp.maximum(tallies, 1.0)[:, None]).astype(jnp.bfloat16)
    columns = tpix // TROWS
    volume = cost_volume.reshape(DEPTH, GROUPS, TROWS, columns).transpose(2, 1, 0, 3)
    hidden = jax.nn.relu(convolve_full(pad_rows(volume), kern_one)).astype(jnp.bfloat16)
    scores = convolve_final(pad_rows(hidden), kern_two)
    return scores


def solution(mesh):
    in_specs = (
        P(("scene", "view"), None, None),
        P(("scene", "view"), None, None),
        P(),
        P(("scene", "view"), None, None),
        P(("scene", "view"), None, None),
        P(("scene", "view"), None),
        P(("scene", "view"), None),
        P(),
        P(),
    )
    out_specs = P(("scene", "view"), None, None)
    return jax.shard_map(body, mesh=mesh, in_specs=in_specs, out_specs=out_specs, check_vma=False)
```

profile of v0, /device:TPU:15, one launch (start us, length us, event | category | flops | bytes accessed | tf_op | source)
XLA Modules:
  0.0 115.5 jit_solution(5268535318414478130)
XLA Ops:
  0.0 1.7 %broadcast_in_dim.18 = bf16[16,32,512]{2,1,0:T(8,128)(2,1)} broadcast(bf16[32,512]{1,0:T(8,128)(2,1)} %bitcast.519), dimensions={1,2} | broadcast | bytes 557056 | tf_op jit(solution)/shard_map/broadcast_in_dim | solution.py:106
  1.7 6.7 %all-to-all-start = ((bf16[16,32,512]{2,1,0:T(8,128)(2,1)}), bf16[16,32,512]{2,1,0:T(8,128)(2,1)S(1)}, u32[]{:S(2)}, u32[]{:S(2)}) async-start(bf16[16,32,512]{2,1,0:T(8,128)(2,1)} %broadcast_in_dim.18), calls=%async_computation | async-start | bytes 1048576 | tf_op jit(solution)/shard_map/all_to_all | solution.py:105
  11.0 20.8 %while.10 = (s32[]{:T(128)}, bf16[8,8,32,512]{3,2,1,0:T(8,128)(2,1)S(1)}, bf16[8,8,4,4]{1,3,2,0:T(4,128)(2,1)S(1)}, s32[8,8,4]{1,0,2:T(8,128)S(1)}, bf16[64,32,1...) while((s32[]{:T(128)}, bf16[8,8,32,512]{3,2,1,0:T(8,128)(2,1)S(1)}, ...), condition=%wide.region_1.2_spmd, body=%wide.region_0.1_spmd.sunk | while | flops 135529568 | bytes 2103897 | solution.py:122
  12.2 1.3 %fusion.280 = bf16[8,8,32,512]{3,2,1,0:T(8,128)(2,1)S(1)} fusion(bf16[8,8,32,512]{3,2,1,0:T(8,128)(2,1)S(1)} %get-tuple-element.117, s32[]{:T(128)} %get-tuple-element.116, bf16[4,128,512]{2,1,0:T(8,128)(2,1)} %get-tuple-element.128, bf16[8,4,32,128]{3,1,2,0:T(4,128)(2,1)S(1)} %convolution_convert_fusion.2), kind=kOutput, calls=%fused_computation.5.clone.1 | convolution fusion | flops 134348800 | bytes 1048580 | tf_op jit(solution)/shard_map/while/body/eval_jaxpr/uwck,wkp->ucp/dot_general | solution.py:118
  14.8 1.3 %fusion.280 = bf16[8,8,32,512]{3,2,1,0:T(8,128)(2,1)S(1)} fusion(bf16[8,8,32,512]{3,2,1,0:T(8,128)(2,1)S(1)} %get-tuple-element.117, s32[]{:T(128)} %get-tuple-element.116, bf16[4,128,512]{2,1,0:T(8,128)(2,1)} %get-tuple-element.128, bf16[8,4,32,128]{3,1,2,0:T(4,128)(2,1)S(1)} %convolution_convert_fusion.2), kind=kOutput, calls=%fused_computation.5.clone.1 | convolution fusion | flops 134348800 | bytes 1048580 | tf_op jit(solution)/shard_map/while/body/eval_jaxpr/uwck,wkp->ucp/dot_general | solution.py:118
  17.4 1.3 %fusion.280 = bf16[8,8,32,512]{3,2,1,0:T(8,128)(2,1)S(1)} fusion(bf16[8,8,32,512]{3,2,1,0:T(8,128)(2,1)S(1)} %get-tuple-element.117, s32[]{:T(128)} %get-tuple-element.116, bf16[4,128,512]{2,1,0:T(8,128)(2,1)} %get-tuple-element.128, bf16[8,4,32,128]{3,1,2,0:T(4,128)(2,1)S(1)} %convolution_convert_fusion.2), kind=kOutput, calls=%fused_computation.5.clone.1 | convolution fusion | flops 134348800 | bytes 1048580 | tf_op jit(solution)/shard_map/while/body/eval_jaxpr/uwck,wkp->ucp/dot_general | solution.py:118
  20.1 1.3 %fusion.280 = bf16[8,8,32,512]{3,2,1,0:T(8,128)(2,1)S(1)} fusion(bf16[8,8,32,512]{3,2,1,0:T(8,128)(2,1)S(1)} %get-tuple-element.117, s32[]{:T(128)} %get-tuple-element.116, bf16[4,128,512]{2,1,0:T(8,128)(2,1)} %get-tuple-element.128, bf16[8,4,32,128]{3,1,2,0:T(4,128)(2,1)S(1)} %convolution_convert_fusion.2), kind=kOutput, calls=%fused_computation.5.clone.1 | convolution fusion | flops 134348800 | bytes 1048580 | tf_op jit(solution)/shard_map/while/body/eval_jaxpr/uwck,wkp->ucp/dot_general | solution.py:118
  22.7 1.3 %fusion.280 = bf16[8,8,32,512]{3,2,1,0:T(8,128)(2,1)S(1)} fusion(bf16[8,8,32,512]{3,2,1,0:T(8,128)(2,1)S(1)} %get-tuple-element.117, s32[]{:T(128)} %get-tuple-element.116, bf16[4,128,512]{2,1,0:T(8,128)(2,1)} %get-tuple-element.128, bf16[8,4,32,128]{3,1,2,0:T(4,128)(2,1)S(1)} %convolution_convert_fusion.2), kind=kOutput, calls=%fused_computation.5.clone.1 | convolution fusion | flops 134348800 | bytes 1048580 | tf_op jit(solution)/shard_map/while/body/eval_jaxpr/uwck,wkp->ucp/dot_general | solution.py:118
  25.3 1.3 %fusion.280 = bf16[8,8,32,512]{3,2,1,0:T(8,128)(2,1)S(1)} fusion(bf16[8,8,32,512]{3,2,1,0:T(8,128)(2,1)S(1)} %get-tuple-element.117, s32[]{:T(128)} %get-tuple-element.116, bf16[4,128,512]{2,1,0:T(8,128)(2,1)} %get-tuple-element.128, bf16[8,4,32,128]{3,1,2,0:T(4,128)(2,1)S(1)} %convolution_convert_fusion.2), kind=kOutput, calls=%fused_computation.5.clone.1 | convolution fusion | flops 134348800 | bytes 1048580 | tf_op jit(solution)/shard_map/while/body/eval_jaxpr/uwck,wkp->ucp/dot_general | solution.py:118
  30.5 1.3 %fusion.280 = bf16[8,8,32,512]{3,2,1,0:T(8,128)(2,1)S(1)} fusion(bf16[8,8,32,512]{3,2,1,0:T(8,128)(2,1)S(1)} %get-tuple-element.117, s32[]{:T(128)} %get-tuple-element.116, bf16[4,128,512]{2,1,0:T(8,128)(2,1)} %get-tuple-element.128, bf16[8,4,32,128]{3,1,2,0:T(4,128)(2,1)S(1)} %convolution_convert_fusion.2), kind=kOutput, calls=%fused_computation.5.clone.1 | convolution fusion | flops 134348800 | bytes 1048580 | tf_op jit(solution)/shard_map/while/body/eval_jaxpr/uwck,wkp->ucp/dot_general | solution.py:118
  31.8 3.0 %reshape.111 = f32[64,8,4,512]{3,2,1,0:T(4,128)} reshape(bf16[8,8,32,512]{3,2,1,0:T(8,128)(2,1)S(1)} %get-tuple-element.37) | data formatting | bytes 6291456 | tf_op jit(solution)/shard_map/convert_element_type | solution.py:125
  35.0 2.5 %mul.20 = f32[16,4,32,512]{3,2,1,0:T(8,128)} broadcast(bf16[16,32,512]{2,1,0:T(8,128)(2,1)S(1)} %all-to-all-done), dimensions={0,2,3} | broadcast | bytes 4718592 | tf_op jit(solution)/shard_map/mul | solution.py:125
  37.5 5.2 %mul.21 = f32[64,8,4,512]{3,2,1,0:T(4,128)} reshape(f32[16,4,32,512]{3,2,1,0:T(8,128)} %mul.20) | data formatting | bytes 8388608 | tf_op jit(solution)/shard_map/mul | solution.py:125
  42.7 7.4 %multiply_reduce_fusion = f32[64,8,512]{2,1,0:T(8,128)S(1)} fusion(f32[64,8,4,512]{3,2,1,0:T(4,128)} %mul.21, f32[64,8,4,512]{3,2,1,0:T(4,128)} %reshape.111), kind=kLoop, calls=%fused_computation.19 | loop fusion | flops 1835008 | bytes 9437184 | tf_op jit(solution)/shard_map/reduce_sum | solution.py:127
  51.7 6.0 %all-to-all-start.1 = ((bf16[16,4,4224]{2,1,0:T(4,128)(2,1)}), bf16[16,4,4224]{2,1,0:T(4,128)(2,1)S(1)}, u32[]{:S(2)}, u32[]{:S(2)}) async-start(bf16[16,4,4224]{2,1,0:T(4,128)(2,1)} %pad_maximum_fusion), calls=%async_computation.1 | async-start | bytes 1081344 | tf_op jit(solution)/shard_map/all_to_all | solution.py:133
  57.8 14.0 %all-to-all-done.1 = bf16[16,4,4224]{2,1,0:T(4,128)(2,1)S(1)} async-done(((bf16[16,4,4224]{2,1,0:T(4,128)(2,1)}), bf16[16,4,4224]{2,1,0:T(4,128)(2,1)S(1)}, u32[]{:S(2)}, u32[]{:S(2)}) %all-to-all-start.1) | async-done | bytes 540704 | tf_op jit(solution)/shard_map/all_to_all | solution.py:133
  73.0 3.6 %collective-permute-start = (bf16[1,8,64,128]{3,1,2,0:T(8,128)(2,1)S(1)}, bf16[1,8,64,128]{3,1,2,0:T(8,128)(2,1)S(1)}, u32[]{:S(2)}, u32[]{:S(2)}) collective-permute-start(bf16[1,8,64,128]{3,1,2,0:T(8,128)(2,1)S(1)} %get-tuple-element.70), channel_id=1, source_target_pairs={{0,1},{1,2},{2,3},{3,4},{4,5},{5,6},{6,7},{7,8},{8,9},{9,10},{10,1... | collective-permute-start | bytes 393224 | tf_op jit(solution)/shard_map/ppermute | solution.py:16
  76.6 2.1 %collective-permute-start.1 = (bf16[1,8,64,128]{3,1,2,0:T(8,128)(2,1)S(1)}, bf16[1,8,64,128]{3,1,2,0:T(8,128)(2,1)S(1)}, u32[]{:S(2)}, u32[]{:S(2)}) collective-permute-start(bf16[1,8,64,128]{3,1,2,0:T(8,128)(2,1)S(1)} %get-tuple-element.71), channel_id=1, source_target_pairs={{1,0},{2,1},{3,2},{4,3},{5,4},{6,5},{7,6},{8,7},{9,8},{10,9},{11,1... | collective-permute-start | bytes 393224 | tf_op jit(solution)/shard_map/ppermute | solution.py:19
  79.1 4.7 %collective-permute-done.1 = bf16[1,8,64,128]{3,1,2,0:T(8,128)(2,1)S(1)} collective-permute-done((bf16[1,8,64,128]{3,1,2,0:T(8,128)(2,1)S(1)}, bf16[1,8,64,128]{3,1,2,0:T(8,128)(2,1)S(1)}, u32[]{:S(2)}, u32[]{:S(2)}) %collective-permute-start.1) | collective-permute-done | bytes 131104 | tf_op jit(solution)/shard_map/ppermute | solution.py:19
  83.8 1.5 %fusion.17 = bf16[6,8,66,130]{3,1,2,0:T(8,128)(2,1)S(1)} fusion(bf16[1,8,64,128]{3,1,2,0:T(8,128)(2,1)S(1)} %collective-permute-done.1, bf16[4,8,64,128]{3,1,2,0:T(8,128)(2,1)S(1)} %bitcast.485, bf16[1,8,64,128]{3,1,2,0:T(8,128)(2,1)S(1)} %collective-permute-done), kind=kLoop, calls=%fused_computation.32 | loop fusion | flops 7824960 | bytes 1610112 | tf_op jit(solution)/shard_map/concatenate | solution.py:20
  95.5 1.9 %collective-permute-start.2 = (bf16[1,8,64,128]{3,1,2,0:T(8,128)(2,1)S(1)}, bf16[1,8,64,128]{3,1,2,0:T(8,128)(2,1)S(1)}, u32[]{:S(2)}, u32[]{:S(2)}) collective-permute-start(bf16[1,8,64,128]{3,1,2,0:T(8,128)(2,1)S(1)} %get-tuple-element.68), channel_id=1, source_target_pairs={{0,1},{1,2},{2,3},{3,4},{4,5},{5,6},{6,7},{7,8},{8,9},{9,10},{10,1... | collective-permute-start | bytes 393224 | tf_op jit(solution)/shard_map/ppermute | solution.py:16
  97.4 2.6 %collective-permute-start.3 = (bf16[1,8,64,128]{3,1,2,0:T(8,128)(2,1)S(1)}, bf16[1,8,64,128]{3,1,2,0:T(8,128)(2,1)S(1)}, u32[]{:S(2)}, u32[]{:S(2)}) collective-permute-start(bf16[1,8,64,128]{3,1,2,0:T(8,128)(2,1)S(1)} %get-tuple-element.69), channel_id=1, source_target_pairs={{1,0},{2,1},{3,2},{4,3},{5,4},{6,5},{7,6},{8,7},{9,8},{10,9},{11,1... | collective-permute-start | bytes 393224 | tf_op jit(solution)/shard_map/ppermute | solution.py:19
  100.4 4.2 %collective-permute-done.3 = bf16[1,8,64,128]{3,1,2,0:T(8,128)(2,1)S(1)} collective-permute-done((bf16[1,8,64,128]{3,1,2,0:T(8,128)(2,1)S(1)}, bf16[1,8,64,128]{3,1,2,0:T(8,128)(2,1)S(1)}, u32[]{:S(2)}, u32[]{:S(2)}) %collective-permute-start.3) | collective-permute-done | bytes 131104 | tf_op jit(solution)/shard_map/ppermute | solution.py:19
  104.6 1.5 %select_maximum_fusion = bf16[6,8,66,130]{3,1,2,0:T(8,128)(2,1)S(1)} fusion(bf16[1,8,64,128]{3,1,2,0:T(8,128)(2,1)S(1)} %collective-permute-done.3, bf16[4,8,64,128]{3,1,2,0:T(8,128)(2,1)S(1)} %fusion.44, bf16[1,8,64,128]{3,1,2,0:T(8,128)(2,1)S(1)} %collective-permute-done.2), kind=kLoop, calls=%fused_computation.23 | loop fusion | flops 7824960 | bytes 1610112 | tf_op jit(solution)/shard_map/concatenate | solution.py:20
  (172 shorter events, 36.4 us)
Async XLA Ops:
  0.0 10.3 %copy-start.3 = (s32[1,64,4]{1,2,0:T(4,128)S(1)}, s32[1,64,4]{1,2,0:T(4,128)}, u32[]{:S(2)}) copy-start(s32[1,64,4]{1,2,0:T(4,128)} %param.15) | copy-start | bytes 3076
  0.0 10.4 %copy-start = (bf16[1,32,8192]{2,1,0:T(8,128)(2,1)S(1)}, bf16[1,32,8192]{2,1,0:T(8,128)(2,1)}, u32[]{:S(2)}) copy-start(bf16[1,32,8192]{2,1,0:T(8,128)(2,1)} %param.11) | copy-start | bytes 1572868
  1.7 9.2 %copy-start.4 = (s32[1,64,4]{1,2,0:T(4,128)S(1)}, s32[1,64,4]{1,2,0:T(4,128)}, u32[]{:S(2)}) copy-start(s32[1,64,4]{1,2,0:T(4,128)} %param.14) | copy-start | bytes 3076
  1.7 33.3 %all-to-all-start = ((bf16[16,32,512]{2,1,0:T(8,128)(2,1)}), bf16[16,32,512]{2,1,0:T(8,128)(2,1)S(1)}, u32[]{:S(2)}, u32[]{:S(2)}) async-start(bf16[16,32,512]{2,1,0:T(8,128)(2,1)} %broadcast_in_dim.18), calls=%async_computation | async-start | bytes 1048576 | tf_op jit(solution)/shard_map/all_to_all | solution.py:105
  31.8 3.0 %copy-start.5 = (s32[1,64]{1,0:T(1,128)S(1)}, s32[1,64]{1,0:T(1,128)}, u32[]{:S(2)}) copy-start(s32[1,64]{1,0:T(1,128)} %param.17) | copy-start | bytes 772
  31.8 3.0 %copy-start.6 = (s32[1,64]{1,0:T(1,128)S(1)}, s32[1,64]{1,0:T(1,128)}, u32[]{:S(2)}) copy-start(s32[1,64]{1,0:T(1,128)} %param.16) | copy-start | bytes 772
  51.7 20.0 %all-to-all-start.1 = ((bf16[16,4,4224]{2,1,0:T(4,128)(2,1)}), bf16[16,4,4224]{2,1,0:T(4,128)(2,1)S(1)}, u32[]{:S(2)}, u32[]{:S(2)}) async-start(bf16[16,4,4224]{2,1,0:T(4,128)(2,1)} %pad_maximum_fusion), calls=%async_computation.1 | async-start | bytes 1081344 | tf_op jit(solution)/shard_map/all_to_all | solution.py:133
  72.5 6.2 %copy-start.2 = (bf16[3,3,3,8,8]{4,3,2,1,0:T(8,128)(2,1)S(1)}, bf16[3,3,3,8,8]{4,3,2,1,0:T(8,128)(2,1)}, u32[]{:S(2)}) copy-start(bf16[3,3,3,8,8]{4,3,2,1,0:T(8,128)(2,1)} %param.18) | copy-start | bytes 10372
  73.0 6.1 %collective-permute-start = (bf16[1,8,64,128]{3,1,2,0:T(8,128)(2,1)S(1)}, bf16[1,8,64,128]{3,1,2,0:T(8,128)(2,1)S(1)}, u32[]{:S(2)}, u32[]{:S(2)}) collective-permute-start(bf16[1,8,64,128]{3,1,2,0:T(8,128)(2,1)S(1)} %get-tuple-element.70), channel_id=1, source_target_pairs={{0,1},{1,2},{2,3},{3,4},{4,5},{5,6},{6,7},{7,8},{8,9},{9,10},{10,1... | collective-permute-start | bytes 393224 | tf_op jit(solution)/shard_map/ppermute | solution.py:16
  76.6 7.2 %collective-permute-start.1 = (bf16[1,8,64,128]{3,1,2,0:T(8,128)(2,1)S(1)}, bf16[1,8,64,128]{3,1,2,0:T(8,128)(2,1)S(1)}, u32[]{:S(2)}, u32[]{:S(2)}) collective-permute-start(bf16[1,8,64,128]{3,1,2,0:T(8,128)(2,1)S(1)} %get-tuple-element.71), channel_id=1, source_target_pairs={{1,0},{2,1},{3,2},{4,3},{5,4},{6,5},{7,6},{8,7},{9,8},{10,9},{11,1... | collective-permute-start | bytes 393224 | tf_op jit(solution)/shard_map/ppermute | solution.py:19
  94.6 5.4 %copy-start.1 = (bf16[3,3,3,8]{3,2,1,0:T(4,128)(2,1)S(1)}, bf16[3,3,3,8]{3,2,1,0:T(4,128)(2,1)}, u32[]{:S(2)}) copy-start(bf16[3,3,3,8]{3,2,1,0:T(4,128)(2,1)} %param.19) | copy-start | bytes 1300
  95.5 4.9 %collective-permute-start.2 = (bf16[1,8,64,128]{3,1,2,0:T(8,128)(2,1)S(1)}, bf16[1,8,64,128]{3,1,2,0:T(8,128)(2,1)S(1)}, u32[]{:S(2)}, u32[]{:S(2)}) collective-permute-start(bf16[1,8,64,128]{3,1,2,0:T(8,128)(2,1)S(1)} %get-tuple-element.68), channel_id=1, source_target_pairs={{0,1},{1,2},{2,3},{3,4},{4,5},{5,6},{6,7},{7,8},{8,9},{9,10},{10,1... | collective-permute-start | bytes 393224 | tf_op jit(solution)/shard_map/ppermute | solution.py:16
  97.4 7.2 %collective-permute-start.3 = (bf16[1,8,64,128]{3,1,2,0:T(8,128)(2,1)S(1)}, bf16[1,8,64,128]{3,1,2,0:T(8,128)(2,1)S(1)}, u32[]{:S(2)}, u32[]{:S(2)}) collective-permute-start(bf16[1,8,64,128]{3,1,2,0:T(8,128)(2,1)S(1)} %get-tuple-element.69), channel_id=1, source_target_pairs={{1,0},{2,1},{3,2},{4,3},{5,4},{6,5},{7,6},{8,7},{9,8},{10,9},{11,1... | collective-permute-start | bytes 393224 | tf_op jit(solution)/shard_map/ppermute | solution.py:19
where the time goes:
time: 116 us; the launch traced here: 115 us
  matrix products  32.3 us (28%)
  starting transfers between devices  23 us (20%)
  waiting for transfers between devices  22.9 us (20%)
  local copies, waits for them, and re-layouts  22.2 us (19%)
  other arithmetic  14 us (12%)
    all_to_all x1, waiting for transfers between devices, body(): lax.all_to_all(payload.reshape(owners, cap, GROUPS * tpix + 128), 'view',...  14 us
    dot_general x8, matrix products, resample(): jnp.einsum('uwck,wkp->ucp', arranged, weight_table, preferred_element_typ...  10.7 us
    dot_general x27, matrix products, convolve_full(): jnp.einsum('rcdw,ce->redw', window, kernel[depth_off, row_off, col_off],...  10.4 us
    ppermute x2, waiting for transfers between devices, with_halo(): lax.ppermute(lax.slice_in_dim(block, 0, width, axis=dim), axis, backward)  8.95 us
    dot_general x27, matrix products, convolve_final(): jnp.einsum('rcdw,c->rdw', window, kernel[depth_off, row_off, col_off], pr...  8.64 us
    mul x2, local copies, waits for them, and re-layouts, body(): ref_all.astype(jnp.float32)[:, None] * warped_all.astype(jnp.float32)  7.69 us
    reduce_sum x1, other arithmetic, body(): products.reshape(units, GROUPS, group_size, tpix).sum(axis=2)  7.41 us
    all_to_all x1, starting transfers between devices, body(): lax.all_to_all(jnp.broadcast_to(ref_feat, (owners,) + ref_feat.shape[1:])...  6.69 us
  transfers between devices with their start and end apart: 6, of which 3 were waited for; matrix products, arithmetic and copies ran while one was open for 23% of the time, Pallas kernels for 0%

commit v1 on v0

--- a/solution.py
+++ b/solution.py
@@ -6,6 +6,29 @@
 GROUPS = 8
 DEPTH = 64
 TROWS = 4
+
+
+def in_blocks(x, dim, count):
+    before, after = (x.shape[:dim], x.shape[dim + 1 :])
+    return jnp.moveaxis(x.reshape(*before, count, -1, *after), dim, 0)
+
+
+def joined_along(tiles, dim):
+    tiles = jnp.moveaxis(tiles, 0, dim)
+    shape = tiles.shape
+    return tiles.reshape(*shape[:dim], shape[dim] * shape[dim + 1], *shape[dim + 2 :])
+
+
+def rotated_exchange(x, axis, split_dim, concat_dim):
+    size, mine = (lax.axis_size(axis), lax.axis_index(axis))
+    blocks = in_blocks(x, split_dim, size)
+    out = blocks
+    for hop in range(1, size):
+        target, source = ((mine + hop) % size, (mine - hop) % size)
+        sent = lax.dynamic_index_in_dim(blocks, target, 0)
+        partner_block = lax.ppermute(sent, axis, [(i, (i + hop) % size) for i in range(size)])
+        out = lax.dynamic_update_slice_in_dim(out, partner_block, source, axis=0)
+    return joined_along(out, concat_dim)
 
 
 def with_halo(block, sides, width):
@@ -102,12 +125,8 @@
     index_groups = src_block[0].reshape(unit_rounds, per_round, slots)
     chosen_groups = chosen.reshape(unit_rounds, per_round, slots, slots)
     group_size = channels // GROUPS
-    ref_all = lax.all_to_all(
-        jnp.broadcast_to(ref_feat, (owners,) + ref_feat.shape[1:]),
-        "view",
-        split_axis=0,
-        concat_axis=0,
-        tiled=True,
+    ref_all = rotated_exchange(
+        jnp.broadcast_to(ref_feat, (owners,) + ref_feat.shape[1:]), "view", 0, 0
     )
 
     def resample(index_rows, chosen_rows):

time: 116 us -> 134 us (1.16)
  starting transfers between devices: 23 us -> 37.2 us
  waiting for transfers between devices: 22.9 us -> 27.1 us
    ppermute x0 -> x15, starting transfers between devices: none -> 20.6 us  [rotated_exchange(): lax.ppermute(sent, axis, [(i, (i + hop) % size) for i in range(size)])]
    all_to_all x1 -> x0, starting transfers between devices: 6.69 us -> none  [body(): lax.all_to_all(jnp.broadcast_to(ref_feat, (owners,) + ref_feat.shape[1:])...]
    ppermute x0 -> x15, waiting for transfers between devices: none -> 4.17 us  [rotated_exchange(): lax.ppermute(sent, axis, [(i, (i + hop) % size) for i in range(size)])]
    broadcast_in_dim x1 -> x0, local copies, waits for them, and re-layouts: 1.67 us -> none  [body(): jnp.broadcast_to(ref_feat, (owners,) + ref_feat.shape[1:])]
  transfers between devices with their start and end apart: 6 -> 20, of which waited for: 3 -> 6; matrix products, arithmetic and copies ran while one was open for 23% -> 20% of each run, Pallas kernels for 0% -> 0%
where the time goes in v1:
time: 134 us; the launch traced here: 133 us
  starting transfers between devices  37.2 us (28%)
  matrix products  32.4 us (24%)
  waiting for transfers between devices  27.1 us (20%)
  local copies, waits for them, and re-layouts  21.7 us (16%)
  other arithmetic  13.3 us (10%)
    ppermute x15, starting transfers between devices, rotated_exchange(): lax.ppermute(sent, axis, [(i, (i + hop) % size) for i in range(size)])  20.6 us
    all_to_all x1, waiting for transfers between devices, body(): lax.all_to_all(payload.reshape(owners, cap, GROUPS * tpix + 128), 'view',...  14 us
    dot_general x8, matrix products, resample(): jnp.einsum('uwck,wkp->ucp', arranged, weight_table, preferred_element_typ...  10.7 us
    dot_general x27, matrix products, convolve_full(): jnp.einsum('rcdw,ce->redw', window, kernel[depth_off, row_off, col_off],...  10.5 us
    ppermute x2, waiting for transfers between devices, with_halo(): lax.ppermute(lax.slice_in_dim(block, 0, width, axis=dim), axis, backward)  8.95 us
    dot_general x27, matrix products, convolve_final(): jnp.einsum('rcdw,c->rdw', window, kernel[depth_off, row_off, col_off], pr...  8.64 us
    mul x2, local copies, waits for them, and re-layouts, body(): ref_all.astype(jnp.float32)[:, None] * warped_all.astype(jnp.float32)  7.75 us
    reduce_sum x1, other arithmetic, body(): products.reshape(units, GROUPS, group_size, tpix).sum(axis=2)  7.32 us
  transfers between devices with their start and end apart: 20, of which 6 were waited for; matrix products, arithmetic and copies ran while one was open for 20% of the time, Pallas kernels for 0%

profile of v1, /device:TPU:15, one launch (start us, length us, event | category | flops | bytes accessed | tf_op | source)
XLA Modules:
  0.0 133.3 jit_solution(7074844341282557759)
XLA Ops:
  0.0 1.9 %collective-permute-start = (bf16[1,1,32,512]{3,2,1,0:T(8,128)(2,1)}, bf16[1,1,32,512]{3,2,1,0:T(8,128)(2,1)S(1)}, u32[]{:S(2)}, u32[]{:S(2)}) collective-permute-start(bf16[1,1,32,512]{3,2,1,0:T(8,128)(2,1)} %bitcast.550), channel_id=1, source_target_pairs={{0,1},{1,2},{2,3},{3,4},{4,5},{5,6},{6,7},{7,8},{8,9},{9,10},{10,1... | collective-permute-start | bytes 98312 | tf_op jit(solution)/shard_map/ppermute | solution.py:29
  4.4 2.7 %collective-permute-start.4 = (bf16[1,1,32,512]{3,2,1,0:T(8,128)(2,1)}, bf16[1,1,32,512]{3,2,1,0:T(8,128)(2,1)S(1)}, u32[]{:S(2)}, u32[]{:S(2)}) collective-permute-start(bf16[1,1,32,512]{3,2,1,0:T(8,128)(2,1)} %bitcast.554), channel_id=1, source_target_pairs={{0,5},{1,6},{2,7},{3,8},{4,9},{5,10},{6,11},{7,12},{8,13},{9,14},{... | collective-permute-start | bytes 98312 | tf_op jit(solution)/shard_map/ppermute | solution.py:29
  10.1 20.8 %while.10 = (s32[]{:T(128)}, bf16[8,8,32,512]{3,2,1,0:T(8,128)(2,1)S(1)}, bf16[8,8,4,4]{1,3,2,0:T(4,128)(2,1)S(1)}, s32[8,8,4]{1,0,2:T(8,128)S(1)}, bf16[64,32,1...) while((s32[]{:T(128)}, bf16[8,8,32,512]{3,2,1,0:T(8,128)(2,1)S(1)}, ...), condition=%wide.region_1.2_spmd, body=%wide.region_0.1_spmd.sunk | while | flops 135529568 | bytes 2103897 | solution.py:141
  31.3 3.0 %reshape.224 = f32[64,8,4,512]{3,2,1,0:T(4,128)} reshape(bf16[8,8,32,512]{3,2,1,0:T(8,128)(2,1)S(1)} %get-tuple-element.37) | data formatting | bytes 6291456 | tf_op jit(solution)/shard_map/convert_element_type | solution.py:144
  34.5 2.3 %collective-permute-start.5 = (bf16[1,1,32,512]{3,2,1,0:T(8,128)(2,1)S(1)}, bf16[1,1,32,512]{3,2,1,0:T(8,128)(2,1)S(1)}, u32[]{:S(2)}, u32[]{:S(2)}) collective-permute-start(bf16[1,1,32,512]{3,2,1,0:T(8,128)(2,1)S(1)} %bitcast.555), channel_id=1, source_target_pairs={{0,6},{1,7},{2,8},{3,9},{4,10},{5,11},{6,12},{7,13},{8,14},{9,15},... | collective-permute-start | bytes 98312 | tf_op jit(solution)/shard_map/ppermute | solution.py:29
  37.6 2.5 %collective-permute-start.8 = (bf16[1,1,32,512]{3,2,1,0:T(8,128)(2,1)S(1)}, bf16[1,1,32,512]{3,2,1,0:T(8,128)(2,1)S(1)}, u32[]{:S(2)}, u32[]{:S(2)}) collective-permute-start(bf16[1,1,32,512]{3,2,1,0:T(8,128)(2,1)S(1)} %bitcast.559), channel_id=1, source_target_pairs={{0,9},{1,10},{2,11},{3,12},{4,13},{5,14},{6,15},{7,0},{8,1},{9,2},... | collective-permute-start | bytes 98312 | tf_op jit(solution)/shard_map/ppermute | solution.py:29
  40.1 2.4 %collective-permute-start.9 = (bf16[1,1,32,512]{3,2,1,0:T(8,128)(2,1)S(1)}, bf16[1,1,32,512]{3,2,1,0:T(8,128)(2,1)S(1)}, u32[]{:S(2)}, u32[]{:S(2)}) collective-permute-start(bf16[1,1,32,512]{3,2,1,0:T(8,128)(2,1)S(1)} %bitcast.560), channel_id=1, source_target_pairs={{0,10},{1,11},{2,12},{3,13},{4,14},{5,15},{6,0},{7,1},{8,2},{9,3},... | collective-permute-start | bytes 98312 | tf_op jit(solution)/shard_map/ppermute | solution.py:29
  44.0 2.4 %collective-permute-start.12 = (bf16[1,1,32,512]{3,2,1,0:T(8,128)(2,1)S(1)}, bf16[1,1,32,512]{3,2,1,0:T(8,128)(2,1)S(1)}, u32[]{:S(2)}, u32[]{:S(2)}) collective-permute-start(bf16[1,1,32,512]{3,2,1,0:T(8,128)(2,1)S(1)} %bitcast.563), channel_id=1, source_target_pairs={{0,13},{1,14},{2,15},{3,0},{4,1},{5,2},{6,3},{7,4},{8,5},{9,6},{10... | collective-permute-start | bytes 98312 | tf_op jit(solution)/shard_map/ppermute | solution.py:29
  46.4 1.8 %collective-permute-start.13 = (bf16[1,1,32,512]{3,2,1,0:T(8,128)(2,1)S(1)}, bf16[1,1,32,512]{3,2,1,0:T(8,128)(2,1)S(1)}, u32[]{:S(2)}, u32[]{:S(2)}) collective-permute-start(bf16[1,1,32,512]{3,2,1,0:T(8,128)(2,1)S(1)} %bitcast.564), channel_id=1, source_target_pairs={{0,14},{1,15},{2,0},{3,1},{4,2},{5,3},{6,4},{7,5},{8,6},{9,7},{10,... | collective-permute-start | bytes 98312 | tf_op jit(solution)/shard_map/ppermute | solution.py:29
  48.5 1.7 %collective-permute-done.13 = bf16[1,1,32,512]{3,2,1,0:T(8,128)(2,1)S(1)} collective-permute-done((bf16[1,1,32,512]{3,2,1,0:T(8,128)(2,1)S(1)}, bf16[1,1,32,512]{3,2,1,0:T(8,128)(2,1)S(1)}, u32[]{:S(2)}, u32[]{:S(2)}) %collective-permute-start.13) | collective-permute-done | bytes 32800 | tf_op jit(solution)/shard_map/ppermute | solution.py:29
  50.1 2.3 %collective-permute-done.14 = bf16[1,1,32,512]{3,2,1,0:T(8,128)(2,1)S(1)} collective-permute-done((bf16[1,1,32,512]{3,2,1,0:T(8,128)(2,1)S(1)}, bf16[1,1,32,512]{3,2,1,0:T(8,128)(2,1)S(1)}, u32[]{:S(2)}, u32[]{:S(2)}) %collective-permute-start.14) | collective-permute-done | bytes 32800 | tf_op jit(solution)/shard_map/ppermute | solution.py:29
  52.5 2.5 %mul.20 = f32[16,4,32,512]{3,2,1,0:T(8,128)} broadcast(bf16[16,32,512]{2,1,0:T(8,128)(2,1)S(1)} %bitcast_dynamic-update-slice_fusion), dimensions={0,2,3} | broadcast | bytes 4718592 | tf_op jit(solution)/shard_map/mul | solution.py:144
  55.0 5.2 %mul.21 = f32[64,8,4,512]{3,2,1,0:T(4,128)} reshape(f32[16,4,32,512]{3,2,1,0:T(8,128)} %mul.20) | data formatting | bytes 8388608 | tf_op jit(solution)/shard_map/mul | solution.py:144
  60.2 7.3 %multiply_reduce_fusion = f32[64,8,512]{2,1,0:T(8,128)S(1)} fusion(f32[64,8,4,512]{3,2,1,0:T(4,128)} %mul.21, f32[64,8,4,512]{3,2,1,0:T(4,128)} %reshape.224), kind=kLoop, calls=%fused_computation.19 | loop fusion | flops 1835008 | bytes 9437184 | tf_op jit(solution)/shard_map/reduce_sum | solution.py:146
  69.2 6.3 %all-to-all-start = ((bf16[16,4,4224]{2,1,0:T(4,128)(2,1)}), bf16[16,4,4224]{2,1,0:T(4,128)(2,1)S(1)}, u32[]{:S(2)}, u32[]{:S(2)}) async-start(bf16[16,4,4224]{2,1,0:T(4,128)(2,1)} %pad_maximum_fusion), calls=%async_computation | async-start | bytes 1081344 | tf_op jit(solution)/shard_map/all_to_all | solution.py:152
  75.5 14.0 %all-to-all-done = bf16[16,4,4224]{2,1,0:T(4,128)(2,1)S(1)} async-done(((bf16[16,4,4224]{2,1,0:T(4,128)(2,1)}), bf16[16,4,4224]{2,1,0:T(4,128)(2,1)S(1)}, u32[]{:S(2)}, u32[]{:S(2)}) %all-to-all-start) | async-done | bytes 540704 | tf_op jit(solution)/shard_map/all_to_all | solution.py:152
  90.8 3.6 %collective-permute-start.15 = (bf16[1,8,64,128]{3,1,2,0:T(8,128)(2,1)S(1)}, bf16[1,8,64,128]{3,1,2,0:T(8,128)(2,1)S(1)}, u32[]{:S(2)}, u32[]{:S(2)}) collective-permute-start(bf16[1,8,64,128]{3,1,2,0:T(8,128)(2,1)S(1)} %get-tuple-element.70), channel_id=1, source_target_pairs={{0,1},{1,2},{2,3},{3,4},{4,5},{5,6},{6,7},{7,8},{8,9},{9,10},{10,1... | collective-permute-start | bytes 393224 | tf_op jit(solution)/shard_map/ppermute | solution.py:39
  94.4 2.1 %collective-permute-start.16 = (bf16[1,8,64,128]{3,1,2,0:T(8,128)(2,1)S(1)}, bf16[1,8,64,128]{3,1,2,0:T(8,128)(2,1)S(1)}, u32[]{:S(2)}, u32[]{:S(2)}) collective-permute-start(bf16[1,8,64,128]{3,1,2,0:T(8,128)(2,1)S(1)} %get-tuple-element.71), channel_id=1, source_target_pairs={{1,0},{2,1},{3,2},{4,3},{5,4},{6,5},{7,6},{8,7},{9,8},{10,9},{11,1... | collective-permute-start | bytes 393224 | tf_op jit(solution)/shard_map/ppermute | solution.py:42
  96.9 4.7 %collective-permute-done.16 = bf16[1,8,64,128]{3,1,2,0:T(8,128)(2,1)S(1)} collective-permute-done((bf16[1,8,64,128]{3,1,2,0:T(8,128)(2,1)S(1)}, bf16[1,8,64,128]{3,1,2,0:T(8,128)(2,1)S(1)}, u32[]{:S(2)}, u32[]{:S(2)}) %collective-permute-start.16) | collective-permute-done | bytes 131104 | tf_op jit(solution)/shard_map/ppermute | solution.py:42
  101.6 1.5 %fusion.17 = bf16[6,8,66,130]{3,1,2,0:T(8,128)(2,1)S(1)} fusion(bf16[1,8,64,128]{3,1,2,0:T(8,128)(2,1)S(1)} %collective-permute-done.16, bf16[4,8,64,128]{3,1,2,0:T(8,128)(2,1)S(1)} %bitcast.516, bf16[1,8,64,128]{3,1,2,0:T(8,128)(2,1)S(1)} %collective-permute-done.15), kind=kLoop, calls=%fused_computation.32 | loop fusion | flops 7824960 | bytes 1610112 | tf_op jit(solution)/shard_map/concatenate | solution.py:43
  113.3 1.9 %collective-permute-start.17 = (bf16[1,8,64,128]{3,1,2,0:T(8,128)(2,1)S(1)}, bf16[1,8,64,128]{3,1,2,0:T(8,128)(2,1)S(1)}, u32[]{:S(2)}, u32[]{:S(2)}) collective-permute-start(bf16[1,8,64,128]{3,1,2,0:T(8,128)(2,1)S(1)} %get-tuple-element.68), channel_id=1, source_target_pairs={{0,1},{1,2},{2,3},{3,4},{4,5},{5,6},{6,7},{7,8},{8,9},{9,10},{10,1... | collective-permute-start | bytes 393224 | tf_op jit(solution)/shard_map/ppermute | solution.py:39
  115.2 2.6 %collective-permute-start.18 = (bf16[1,8,64,128]{3,1,2,0:T(8,128)(2,1)S(1)}, bf16[1,8,64,128]{3,1,2,0:T(8,128)(2,1)S(1)}, u32[]{:S(2)}, u32[]{:S(2)}) collective-permute-start(bf16[1,8,64,128]{3,1,2,0:T(8,128)(2,1)S(1)} %get-tuple-element.69), channel_id=1, source_target_pairs={{1,0},{2,1},{3,2},{4,3},{5,4},{6,5},{7,6},{8,7},{9,8},{10,9},{11,1... | collective-permute-start | bytes 393224 | tf_op jit(solution)/shard_map/ppermute | solution.py:42
  118.2 4.2 %collective-permute-done.18 = bf16[1,8,64,128]{3,1,2,0:T(8,128)(2,1)S(1)} collective-permute-done((bf16[1,8,64,128]{3,1,2,0:T(8,128)(2,1)S(1)}, bf16[1,8,64,128]{3,1,2,0:T(8,128)(2,1)S(1)}, u32[]{:S(2)}, u32[]{:S(2)}) %collective-permute-start.18) | collective-permute-done | bytes 131104 | tf_op jit(solution)/shard_map/ppermute | solution.py:42
  122.4 1.5 %select_maximum_fusion = bf16[6,8,66,130]{3,1,2,0:T(8,128)(2,1)S(1)} fusion(bf16[1,8,64,128]{3,1,2,0:T(8,128)(2,1)S(1)} %collective-permute-done.18, bf16[4,8,64,128]{3,1,2,0:T(8,128)(2,1)S(1)} %fusion.44, bf16[1,8,64,128]{3,1,2,0:T(8,128)(2,1)S(1)} %collective-permute-done.17), kind=kLoop, calls=%fused_computation.23 | loop fusion | flops 7824960 | bytes 1610112 | tf_op jit(solution)/shard_map/concatenate | solution.py:43
  (215 shorter events, 51.4 us)
Async XLA Ops:
  0.0 8.6 %copy-start.3 = (s32[1,64,4]{1,2,0:T(4,128)S(1)}, s32[1,64,4]{1,2,0:T(4,128)}, u32[]{:S(2)}) copy-start(s32[1,64,4]{1,2,0:T(4,128)} %param.15) | copy-start | bytes 3076
  0.0 9.2 %copy-start.6 = (s32[1,64]{1,0:T(1,128)S(1)}, s32[1,64]{1,0:T(1,128)}, u32[]{:S(2)}) copy-start(s32[1,64]{1,0:T(1,128)} %param.16) | copy-start | bytes 772
  0.0 10.0 %copy-start.4 = (s32[1,64,4]{1,2,0:T(4,128)S(1)}, s32[1,64,4]{1,2,0:T(4,128)}, u32[]{:S(2)}) copy-start(s32[1,64,4]{1,2,0:T(4,128)} %param.14) | copy-start | bytes 3076
  0.0 34.5 %collective-permute-start = (bf16[1,1,32,512]{3,2,1,0:T(8,128)(2,1)}, bf16[1,1,32,512]{3,2,1,0:T(8,128)(2,1)S(1)}, u32[]{:S(2)}, u32[]{:S(2)}) collective-permute-start(bf16[1,1,32,512]{3,2,1,0:T(8,128)(2,1)} %bitcast.550), channel_id=1, source_target_pairs={{0,1},{1,2},{2,3},{3,4},{4,5},{5,6},{6,7},{7,8},{8,9},{9,10},{10,1... | collective-permute-start | bytes 98312 | tf_op jit(solution)/shard_map/ppermute | solution.py:29
  1.9 35.0 %collective-permute-start.1 = (bf16[1,1,32,512]{3,2,1,0:T(8,128)(2,1)}, bf16[1,1,32,512]{3,2,1,0:T(8,128)(2,1)S(1)}, u32[]{:S(2)}, u32[]{:S(2)}) collective-permute-start(bf16[1,1,32,512]{3,2,1,0:T(8,128)(2,1)} %bitcast.551), channel_id=1, source_target_pairs={{0,2},{1,3},{2,4},{3,5},{4,6},{5,7},{6,8},{7,9},{8,10},{9,11},{10,... | collective-permute-start | bytes 98312 | tf_op jit(solution)/shard_map/ppermute | solution.py:29
  3.1 33.9 %collective-permute-start.2 = (bf16[1,1,32,512]{3,2,1,0:T(8,128)(2,1)}, bf16[1,1,32,512]{3,2,1,0:T(8,128)(2,1)S(1)}, u32[]{:S(2)}, u32[]{:S(2)}) collective-permute-start(bf16[1,1,32,512]{3,2,1,0:T(8,128)(2,1)} %bitcast.552), channel_id=1, source_target_pairs={{0,3},{1,4},{2,5},{3,6},{4,7},{5,8},{6,9},{7,10},{8,11},{9,12},{10... | collective-permute-start | bytes 98312 | tf_op jit(solution)/shard_map/ppermute | solution.py:29
  3.5 34.1 %collective-permute-start.3 = (bf16[1,1,32,512]{3,2,1,0:T(8,128)(2,1)}, bf16[1,1,32,512]{3,2,1,0:T(8,128)(2,1)S(1)}, u32[]{:S(2)}, u32[]{:S(2)}) collective-permute-start(bf16[1,1,32,512]{3,2,1,0:T(8,128)(2,1)} %bitcast.553), channel_id=1, source_target_pairs={{0,4},{1,5},{2,6},{3,7},{4,8},{5,9},{6,10},{7,11},{8,12},{9,13},{1... | collective-permute-start | bytes 98312 | tf_op jit(solution)/shard_map/ppermute | solution.py:29
  4.4 35.7 %collective-permute-start.4 = (bf16[1,1,32,512]{3,2,1,0:T(8,128)(2,1)}, bf16[1,1,32,512]{3,2,1,0:T(8,128)(2,1)S(1)}, u32[]{:S(2)}, u32[]{:S(2)}) collective-permute-start(bf16[1,1,32,512]{3,2,1,0:T(8,128)(2,1)} %bitcast.554), channel_id=1, source_target_pairs={{0,5},{1,6},{2,7},{3,8},{4,9},{5,10},{6,11},{7,12},{8,13},{9,14},{... | collective-permute-start | bytes 98312 | tf_op jit(solution)/shard_map/ppermute | solution.py:29
  10.1 20.8 %copy-start.5 = (s32[1,64]{1,0:T(1,128)S(1)}, s32[1,64]{1,0:T(1,128)}, u32[]{:S(2)}) copy-start(s32[1,64]{1,0:T(1,128)} %param.17) | copy-start | bytes 772
  34.5 8.0 %collective-permute-start.5 = (bf16[1,1,32,512]{3,2,1,0:T(8,128)(2,1)S(1)}, bf16[1,1,32,512]{3,2,1,0:T(8,128)(2,1)S(1)}, u32[]{:S(2)}, u32[]{:S(2)}) collective-permute-start(bf16[1,1,32,512]{3,2,1,0:T(8,128)(2,1)S(1)} %bitcast.555), channel_id=1, source_target_pairs={{0,6},{1,7},{2,8},{3,9},{4,10},{5,11},{6,12},{7,13},{8,14},{9,15},... | collective-permute-start | bytes 98312 | tf_op jit(solution)/shard_map/ppermute | solution.py:29
  36.9 5.7 %collective-permute-start.6 = (bf16[1,1,32,512]{3,2,1,0:T(8,128)(2,1)S(1)}, bf16[1,1,32,512]{3,2,1,0:T(8,128)(2,1)S(1)}, u32[]{:S(2)}, u32[]{:S(2)}) collective-permute-start(bf16[1,1,32,512]{3,2,1,0:T(8,128)(2,1)S(1)} %bitcast.557), channel_id=1, source_target_pairs={{0,7},{1,8},{2,9},{3,10},{4,11},{5,12},{6,13},{7,14},{8,15},{9,0},... | collective-permute-start | bytes 98312 | tf_op jit(solution)/shard_map/ppermute | solution.py:29
  37.0 7.0 %collective-permute-start.7 = (bf16[1,1,32,512]{3,2,1,0:T(8,128)(2,1)S(1)}, bf16[1,1,32,512]{3,2,1,0:T(8,128)(2,1)S(1)}, u32[]{:S(2)}, u32[]{:S(2)}) collective-permute-start(bf16[1,1,32,512]{3,2,1,0:T(8,128)(2,1)S(1)} %bitcast.558), channel_id=1, source_target_pairs={{0,8},{1,9},{2,10},{3,11},{4,12},{5,13},{6,14},{7,15},{8,0},{9,1},... | collective-permute-start | bytes 98312 | tf_op jit(solution)/shard_map/ppermute | solution.py:29
  37.6 8.8 %collective-permute-start.8 = (bf16[1,1,32,512]{3,2,1,0:T(8,128)(2,1)S(1)}, bf16[1,1,32,512]{3,2,1,0:T(8,128)(2,1)S(1)}, u32[]{:S(2)}, u32[]{:S(2)}) collective-permute-start(bf16[1,1,32,512]{3,2,1,0:T(8,128)(2,1)S(1)} %bitcast.559), channel_id=1, source_target_pairs={{0,9},{1,10},{2,11},{3,12},{4,13},{5,14},{6,15},{7,0},{8,1},{9,2},... | collective-permute-start | bytes 98312 | tf_op jit(solution)/shard_map/ppermute | solution.py:29
  40.1 8.1 %collective-permute-start.9 = (bf16[1,1,32,512]{3,2,1,0:T(8,128)(2,1)S(1)}, bf16[1,1,32,512]{3,2,1,0:T(8,128)(2,1)S(1)}, u32[]{:S(2)}, u32[]{:S(2)}) collective-permute-start(bf16[1,1,32,512]{3,2,1,0:T(8,128)(2,1)S(1)} %bitcast.560), channel_id=1, source_target_pairs={{0,10},{1,11},{2,12},{3,13},{4,14},{5,15},{6,0},{7,1},{8,2},{9,3},... | collective-permute-start | bytes 98312 | tf_op jit(solution)/shard_map/ppermute | solution.py:29
  42.5 5.8 %collective-permute-start.10 = (bf16[1,1,32,512]{3,2,1,0:T(8,128)(2,1)S(1)}, bf16[1,1,32,512]{3,2,1,0:T(8,128)(2,1)S(1)}, u32[]{:S(2)}, u32[]{:S(2)}) collective-permute-start(bf16[1,1,32,512]{3,2,1,0:T(8,128)(2,1)S(1)} %bitcast.561), channel_id=1, source_target_pairs={{0,11},{1,12},{2,13},{3,14},{4,15},{5,0},{6,1},{7,2},{8,3},{9,4},{... | collective-permute-start | bytes 98312 | tf_op jit(solution)/shard_map/ppermute | solution.py:29
  42.6 5.7 %collective-permute-start.11 = (bf16[1,1,32,512]{3,2,1,0:T(8,128)(2,1)S(1)}, bf16[1,1,32,512]{3,2,1,0:T(8,128)(2,1)S(1)}, u32[]{:S(2)}, u32[]{:S(2)}) collective-permute-start(bf16[1,1,32,512]{3,2,1,0:T(8,128)(2,1)S(1)} %bitcast.562), channel_id=1, source_target_pairs={{0,12},{1,13},{2,14},{3,15},{4,0},{5,1},{6,2},{7,3},{8,4},{9,5},{1... | collective-permute-start | bytes 98312 | tf_op jit(solution)/shard_map/ppermute | solution.py:29
  44.0 4.4 %collective-permute-start.12 = (bf16[1,1,32,512]{3,2,1,0:T(8,128)(2,1)S(1)}, bf16[1,1,32,512]{3,2,1,0:T(8,128)(2,1)S(1)}, u32[]{:S(2)}, u32[]{:S(2)}) collective-permute-start(bf16[1,1,32,512]{3,2,1,0:T(8,128)(2,1)S(1)} %bitcast.563), channel_id=1, source_target_pairs={{0,13},{1,14},{2,15},{3,0},{4,1},{5,2},{6,3},{7,4},{8,5},{9,6},{10... | collective-permute-start | bytes 98312 | tf_op jit(solution)/shard_map/ppermute | solution.py:29
  46.4 3.7 %collective-permute-start.13 = (bf16[1,1,32,512]{3,2,1,0:T(8,128)(2,1)S(1)}, bf16[1,1,32,512]{3,2,1,0:T(8,128)(2,1)S(1)}, u32[]{:S(2)}, u32[]{:S(2)}) collective-permute-start(bf16[1,1,32,512]{3,2,1,0:T(8,128)(2,1)S(1)} %bitcast.564), channel_id=1, source_target_pairs={{0,14},{1,15},{2,0},{3,1},{4,2},{5,3},{6,4},{7,5},{8,6},{9,7},{10,... | collective-permute-start | bytes 98312 | tf_op jit(solution)/shard_map/ppermute | solution.py:29
  48.2 4.3 %collective-permute-start.14 = (bf16[1,1,32,512]{3,2,1,0:T(8,128)(2,1)S(1)}, bf16[1,1,32,512]{3,2,1,0:T(8,128)(2,1)S(1)}, u32[]{:S(2)}, u32[]{:S(2)}) collective-permute-start(bf16[1,1,32,512]{3,2,1,0:T(8,128)(2,1)S(1)} %bitcast.565), channel_id=1, source_target_pairs={{0,15},{1,0},{2,1},{3,2},{4,3},{5,4},{6,5},{7,6},{8,7},{9,8},{10,9... | collective-permute-start | bytes 98312 | tf_op jit(solution)/shard_map/ppermute | solution.py:29
  69.2 20.3 %all-to-all-start = ((bf16[16,4,4224]{2,1,0:T(4,128)(2,1)}), bf16[16,4,4224]{2,1,0:T(4,128)(2,1)S(1)}, u32[]{:S(2)}, u32[]{:S(2)}) async-start(bf16[16,4,4224]{2,1,0:T(4,128)(2,1)} %pad_maximum_fusion), calls=%async_computation | async-start | bytes 1081344 | tf_op jit(solution)/shard_map/all_to_all | solution.py:152
  90.8 6.1 %collective-permute-start.15 = (bf16[1,8,64,128]{3,1,2,0:T(8,128)(2,1)S(1)}, bf16[1,8,64,128]{3,1,2,0:T(8,128)(2,1)S(1)}, u32[]{:S(2)}, u32[]{:S(2)}) collective-permute-start(bf16[1,8,64,128]{3,1,2,0:T(8,128)(2,1)S(1)} %get-tuple-element.70), channel_id=1, source_target_pairs={{0,1},{1,2},{2,3},{3,4},{4,5},{5,6},{6,7},{7,8},{8,9},{9,10},{10,1... | collective-permute-start | bytes 393224 | tf_op jit(solution)/shard_map/ppermute | solution.py:39
  94.4 7.2 %collective-permute-start.16 = (bf16[1,8,64,128]{3,1,2,0:T(8,128)(2,1)S(1)}, bf16[1,8,64,128]{3,1,2,0:T(8,128)(2,1)S(1)}, u32[]{:S(2)}, u32[]{:S(2)}) collective-permute-start(bf16[1,8,64,128]{3,1,2,0:T(8,128)(2,1)S(1)} %get-tuple-element.71), channel_id=1, source_target_pairs={{1,0},{2,1},{3,2},{4,3},{5,4},{6,5},{7,6},{8,7},{9,8},{10,9},{11,1... | collective-permute-start | bytes 393224 | tf_op jit(solution)/shard_map/ppermute | solution.py:42
  113.3 4.9 %collective-permute-start.17 = (bf16[1,8,64,128]{3,1,2,0:T(8,128)(2,1)S(1)}, bf16[1,8,64,128]{3,1,2,0:T(8,128)(2,1)S(1)}, u32[]{:S(2)}, u32[]{:S(2)}) collective-permute-start(bf16[1,8,64,128]{3,1,2,0:T(8,128)(2,1)S(1)} %get-tuple-element.68), channel_id=1, source_target_pairs={{0,1},{1,2},{2,3},{3,4},{4,5},{5,6},{6,7},{7,8},{8,9},{9,10},{10,1... | collective-permute-start | bytes 393224 | tf_op jit(solution)/shard_map/ppermute | solution.py:39
  115.2 7.2 %collective-permute-start.18 = (bf16[1,8,64,128]{3,1,2,0:T(8,128)(2,1)S(1)}, bf16[1,8,64,128]{3,1,2,0:T(8,128)(2,1)S(1)}, u32[]{:S(2)}, u32[]{:S(2)}) collective-permute-start(bf16[1,8,64,128]{3,1,2,0:T(8,128)(2,1)S(1)} %get-tuple-element.69), channel_id=1, source_target_pairs={{1,0},{2,1},{3,2},{4,3},{5,4},{6,5},{7,6},{8,7},{9,8},{10,9},{11,1... | collective-permute-start | bytes 393224 | tf_op jit(solution)/shard_map/ppermute | solution.py:42
  (3 other events, 14.9 us)
